TPU v7x, 128 devices: a whole 4x4x4 slice. The times are simulated.
128 devices in a mesh: leaf: 16 (over z, x), panel: 8 (over y, core).
Axes of the slice: x: 4, y: 4, z: 4, core: 2. Of those that a mesh axis runs over, the one named last changes fastest.
Arguments:
- child_front: float32 [16, 2048, 2048], P('leaf', 'panel'), as said below
- child_panel: bfloat16 [16, 2048, 4096], P('leaf'), may hold values from -0.03125 to 0.03125
- parent_front: float32 [4096, 4096], P('leaf', 'panel'), as said below
- tile_map: int32 [16, 8], P('leaf'), may hold values from 0 to 15, as said below
- tile_count: int32 [16], P('leaf'), may hold values from 2 to 8, as said below
Outputs:
- eliminated: float32 [4096, 4096], P('leaf', 'panel')
Inputs may be any that keep to these rules, and one draw needn't show every extreme that they name: `tile_count`: some child has 8 live tiles and some child has 2. `tile_map`: for child c the first tile_count[c] entries are distinct and rising; the other entries are 0. Each child's block is symmetric, and child_front[c] - child_panel[c] child_panel[c]^T is positive definite. `parent_front`: symmetric positive definite.
All inputs are finite; a program needn't handle non-finite values.
Results may differ from a plain program's by a relative error of at most 0.0003.
Values sent between devices are 32-bit elements; how exact they have to be, the bound alone decides.
No kernel may reach another device: no remote copies, remote signals or barrier semaphores. Data moves between devices by JAX's collectives and lax.ppermute only.
A program may use at most 128 MiB of HBM per device.

v0:
```python
import jax
import jax.numpy as jnp
from jax import lax
from jax.sharding import PartitionSpec as P

TILE = 256
NF = 4096
CB = 2048
STEPS = 4


def spread(array, axis, root):
    mine = lax.axis_index(axis) == root
    return lax.psum(jnp.where(mine, array, jnp.zeros_like(array)), axis)


def finish_rows(block, row_index, factor, pivot_start):
    solved = lax.linalg.triangular_solve(
        factor, block, left_side=False, lower=True, transpose_a=True
    )
    offset = jnp.clip(row_index - pivot_start, 0, TILE - 1)
    own_rows = jnp.take(factor, offset, axis=0)
    inside = (row_index >= pivot_start) & (row_index < pivot_start + TILE)
    kept = jnp.where(inside[:, None], own_rows, solved)
    return jnp.where(row_index[:, None] < pivot_start, 0.0, kept)


def shards(child_front, child_panel, parent_front, tile_map, tile_count):
    highest = lax.Precision.HIGHEST
    panel_count = lax.axis_size("panel")
    leaf_id = lax.axis_index("leaf")
    panel_id = lax.axis_index("panel")
    tiles_child = CB // TILE
    tiles_front = NF // TILE
    pivot_span = STEPS * TILE
    child_rows = child_front.shape[1]
    height = parent_front.shape[0]
    col_width = parent_front.shape[1]
    panel_all = child_panel[0]
    own_panel = lax.dynamic_slice_in_dim(panel_all, panel_id * child_rows, child_rows, 0)
    update = child_front[0] - lax.dot_general(
        own_panel, panel_all, (((1,), (1,)), ((), ())), preferred_element_type=jnp.float32
    )
    mapped = tile_map[0]
    live_tiles = jnp.arange(tiles_child, dtype=jnp.int32) < tile_count[0]
    everywhere = jnp.arange(tiles_front, dtype=jnp.int32)
    chosen = ((mapped[None, :] == everywhere[:, None]) & live_tiles[None, :]).astype(jnp.float32)
    placed = jnp.einsum(
        "rtb,ft->rfb", update.reshape(child_rows, tiles_child, TILE), chosen, precision=highest
    )
    placed = placed.reshape(child_rows, panel_count, col_width)
    moved_cols = lax.all_to_all(placed, "panel", split_axis=1, concat_axis=0, tiled=True)
    column_tiles = moved_cols.reshape(tiles_child, TILE, col_width)
    targets = jnp.arange(lax.axis_size("leaf") * height // TILE, dtype=jnp.int32)
    picked = ((mapped[None, :] == targets[:, None]) & live_tiles[None, :]).astype(jnp.float32)
    front_block = parent_front + lax.psum_scatter(
        jnp.einsum("ft,tbc->fbc", picked, column_tiles, precision=highest).reshape(
            lax.axis_size("leaf") * height, col_width
        ),
        "leaf",
        scatter_dimension=0,
        tiled=True,
    )
    global_rows = leaf_id * height + jnp.arange(height, dtype=jnp.int32)
    global_cols = panel_id * col_width + jnp.arange(col_width, dtype=jnp.int32)
    col_tiles = col_width // TILE
    for pivot_step in range(STEPS):
        source_panel = pivot_step // col_tiles
        local_start = pivot_step % col_tiles * TILE
        pivot_start = pivot_step * TILE
        source = front_block[:, local_start : local_start + TILE]
        column = spread(source, "panel", source_panel)
        full_column = lax.all_gather(column, "leaf", axis=0, tiled=True)
        factor = jnp.linalg.cholesky(full_column[pivot_start : pivot_start + TILE])
        own_factor = finish_rows(column, global_rows, factor, pivot_start)
        col_factor = finish_rows(
            lax.dynamic_slice_in_dim(full_column, panel_id * col_width, col_width, 0),
            global_cols,
            factor,
            pivot_start,
        )
        front_block = front_block - lax.dot_general(
            own_factor,
            col_factor,
            (((1,), (1,)), ((), ())),
            precision=highest,
            preferred_element_type=jnp.float32,
        )
        replaced = jnp.where(
            panel_id == source_panel, own_factor, front_block[:, local_start : local_start + TILE]
        )
        front_block = front_block.at[:, local_start : local_start + TILE].set(replaced)
    upper_zone = (global_rows[:, None] < pivot_span) & (global_cols[None, :] >= pivot_span)
    return jnp.where(upper_zone, 0.0, front_block)


def solution(mesh):
    placed = (
        P("leaf", "panel", None),
        P("leaf", None, None),
        P("leaf", "panel"),
        P("leaf", None),
        P("leaf"),
    )
    return jax.shard_map(
        shards, mesh=mesh, in_specs=placed, out_specs=P("leaf", "panel"), check_vma=False
    )
```

profile of v0, /device:TPU:0, one launch (start us, length us, event | category | flops | bytes accessed | tf_op | source)
XLA Modules:
  0.0 964.4 jit_solution(7068307118465232745)
XLA Ops:
  6.5 11.5 %fusion.2 = f32[256,2048]{1,0:T(8,128)S(1)} fusion(bf16[1,2048,4096]{2,1,0:T(8,128)(2,1)} %param.23, f32[1,256,2048]{2,1,0:T(8,128)} %param.22, s32[]{:T(128)S(6)} %select_n.120), kind=kOutput, calls=%fused_computation.18 | convolution fusion | flops 4295491584 | bytes 23068676 | tf_op jit(solution)/shard_map/dot_general | solution.py:41
  33.0 54.3 %all_to_all.15 = f32[256,8,512]{2,0,1:T(8,128)} all-to-all(f32[256,8,512]{2,0,1:T(8,128)S(1)} %copy.25), channel_id=1, replica_groups=mesh['leaf'=16,'panel'=8] {'panel'}, dimensions={1} | all-to-all | bytes 8388608 | tf_op jit(solution)/shard_map/all_to_all | solution.py:52
  98.4 11.3 %copy.54 = f32[64,8,16,256]{3,1,2,0:T(8,128)} copy(f32[64,8,16,256]{3,2,1,0:T(8,128)S(1)} %bitcast.200) | data formatting | bytes 16777216
  110.9 85.6 %reduce-scatter.2.cloned.1.call-done = f32[256,512]{0,1:T(8,128)} async-done(((f32[4096,512]{0,1:T(8,128)}), f32[256,512]{0,1:T(8,128)}) %reduce-scatter.2.cloned.1.call-update) | async-done | bytes 524304 | tf_op jit(solution)/shard_map/reduce_scatter | solution.py:56
  198.4 60.0 %all-reduce.6.cloned.1.call-done = f32[256,256]{0,1:T(8,128)} async-done(((f32[256,256]{0,1:T(8,128)}), f32[256,256]{0,1:T(8,128)}) %all-reduce.6.cloned.1.call-update) | async-done | bytes 262160 | tf_op jit(solution)/shard_map/psum | solution.py:14
  259.5 57.1 %all-gather.5.cloned.1.call-done = f32[4096,256]{0,1:T(8,128)} async-done(((f32[256,256]{0,1:T(8,128)}), f32[4096,256]{0,1:T(8,128)}) %all-gather.5.cloned.1.call-update) | async-done | bytes 4194320 | tf_op jit(solution)/shard_map/all_gather | solution.py:73
  318.7 11.7 %cholesky.214 = f32[128,128]{1,0:T(8,128)S(1)} custom-call(f32[128,128]{1,0:T(8,128)S(1)} %cholesky.346), custom_call_target="Cholesky" | custom-call | tf_op jit(solution)/shard_map/jit(cholesky)/cholesky | solution.py:74
  340.7 11.7 %cholesky.231 = f32[128,128]{1,0:T(8,128)S(1)} custom-call(f32[128,128]{1,0:T(8,128)S(1)} %convolution_subtract_fusion.15), custom_call_target="Cholesky" | custom-call | tf_op jit(solution)/shard_map/jit(cholesky)/cholesky | solution.py:74
  358.8 20.1 %custom-call.24 = f32[2,128,128]{1,2,0:T(8,128)S(1)} custom-call(f32[2,128,128]{2,1,0:T(8,128)S(1)} %get-tuple-element.110), custom_call_target="InvertDiagBlocksLowerTriangular" | custom-call | tf_op jit(solution)/shard_map/triangular_solve/custom-call.0 | solution.py:18
  388.4 59.7 %all-reduce.8.cloned.1.call-done = f32[256,256]{0,1:T(8,128)} async-done(((f32[256,256]{0,1:T(8,128)}), f32[256,256]{0,1:T(8,128)}) %all-reduce.8.cloned.1.call-update) | async-done | bytes 262160 | tf_op jit(solution)/shard_map/psum | solution.py:14
  448.5 57.6 %all-gather.7.cloned.1.call-done = f32[4096,256]{0,1:T(8,128)} async-done(((f32[256,256]{0,1:T(8,128)}), f32[4096,256]{0,1:T(8,128)}) %all-gather.7.cloned.1.call-update) | async-done | bytes 4194320 | tf_op jit(solution)/shard_map/all_gather | solution.py:73
  508.3 11.7 %cholesky.248 = f32[128,128]{1,0:T(8,128)S(1)} custom-call(f32[128,128]{1,0:T(8,128)S(1)} %cholesky.349), custom_call_target="Cholesky" | custom-call | tf_op jit(solution)/shard_map/jit(cholesky)/cholesky | solution.py:74
  530.3 11.7 %cholesky.265 = f32[128,128]{1,0:T(8,128)S(1)} custom-call(f32[128,128]{1,0:T(8,128)S(1)} %convolution_subtract_fusion.14), custom_call_target="Cholesky" | custom-call | tf_op jit(solution)/shard_map/jit(cholesky)/cholesky | solution.py:74
  549.3 19.7 %custom-call.27 = f32[2,128,128]{1,2,0:T(8,128)S(1)} custom-call(f32[2,128,128]{2,1,0:T(8,128)S(1)} %get-tuple-element.112), custom_call_target="InvertDiagBlocksLowerTriangular" | custom-call | tf_op jit(solution)/shard_map/triangular_solve/custom-call.0 | solution.py:18
  577.8 59.7 %all-reduce.10.cloned.1.call-done = f32[256,256]{0,1:T(8,128)} async-done(((f32[256,256]{0,1:T(8,128)}), f32[256,256]{0,1:T(8,128)}) %all-reduce.10.cloned.1.call-update) | async-done | bytes 262160 | tf_op jit(solution)/shard_map/psum | solution.py:14
  637.9 57.7 %all-gather.9.cloned.1.call-done = f32[4096,256]{0,1:T(8,128)} async-done(((f32[256,256]{0,1:T(8,128)}), f32[4096,256]{0,1:T(8,128)}) %all-gather.9.cloned.1.call-update) | async-done | bytes 4194320 | tf_op jit(solution)/shard_map/all_gather | solution.py:73
  697.7 11.7 %cholesky.282 = f32[128,128]{1,0:T(8,128)S(1)} custom-call(f32[128,128]{1,0:T(8,128)S(1)} %cholesky.352), custom_call_target="Cholesky" | custom-call | tf_op jit(solution)/shard_map/jit(cholesky)/cholesky | solution.py:74
  719.8 11.7 %cholesky.299 = f32[128,128]{1,0:T(8,128)S(1)} custom-call(f32[128,128]{1,0:T(8,128)S(1)} %convolution_subtract_fusion.13), custom_call_target="Cholesky" | custom-call | tf_op jit(solution)/shard_map/jit(cholesky)/cholesky | solution.py:74
  739.0 19.7 %custom-call.30 = f32[2,128,128]{1,2,0:T(8,128)S(1)} custom-call(f32[2,128,128]{2,1,0:T(8,128)S(1)} %get-tuple-element.114), custom_call_target="InvertDiagBlocksLowerTriangular" | custom-call | tf_op jit(solution)/shard_map/triangular_solve/custom-call.0 | solution.py:18
  768.4 59.5 %all-reduce.12.cloned.1.call-done = f32[256,256]{0,1:T(8,128)} async-done(((f32[256,256]{0,1:T(8,128)}), f32[256,256]{0,1:T(8,128)}) %all-reduce.12.cloned.1.call-update) | async-done | bytes 262160 | tf_op jit(solution)/shard_map/psum | solution.py:14
  828.0 58.0 %all-gather.11.cloned.1.call-done = f32[4096,256]{0,1:T(8,128)} async-done(((f32[256,256]{0,1:T(8,128)}), f32[4096,256]{0,1:T(8,128)}) %all-gather.11.cloned.1.call-update) | async-done | bytes 4194320 | tf_op jit(solution)/shard_map/all_gather | solution.py:73
  888.1 11.7 %cholesky.316 = f32[128,128]{1,0:T(8,128)S(1)} custom-call(f32[128,128]{1,0:T(8,128)S(1)} %cholesky.355), custom_call_target="Cholesky" | custom-call | tf_op jit(solution)/shard_map/jit(cholesky)/cholesky | solution.py:74
  910.2 11.7 %cholesky.333 = f32[128,128]{1,0:T(8,128)S(1)} custom-call(f32[128,128]{1,0:T(8,128)S(1)} %convolution_subtract_fusion.12), custom_call_target="Cholesky" | custom-call | tf_op jit(solution)/shard_map/jit(cholesky)/cholesky | solution.py:74
  928.8 19.7 %custom-call.33 = f32[2,128,128]{1,2,0:T(8,128)S(1)} custom-call(f32[2,128,128]{2,1,0:T(8,128)S(1)} %get-tuple-element.116), custom_call_target="InvertDiagBlocksLowerTriangular" | custom-call | tf_op jit(solution)/shard_map/triangular_solve/custom-call.0 | solution.py:18
  (210 shorter events, 155.6 us)
Async XLA Ops:
  6.5 190.0 %reduce-scatter.2.cloned.1.call-start = ((), (), s32[]{:S(2)}) async-start(), calls=%async_computation.2 | async-start | bytes 8912896 | tf_op jit(solution)/shard_map/reduce_scatter | solution.py:56
  18.0 1.6 copy-start.5
  109.7 1.0 copy-start.4
  109.7 148.7 %all-reduce.6.cloned.1.call-start = ((), (), s32[]{:S(2)}) async-start(), calls=%async_computation.3 | async-start | bytes 524288 | tf_op jit(solution)/shard_map/psum | solution.py:14
  198.3 118.2 %all-gather.5.cloned.1.call-start = ((), (), s32[]{:S(2)}) async-start(), calls=%async_computation.4 | async-start | bytes 4456448 | tf_op jit(solution)/shard_map/all_gather | solution.py:73
  258.4 120.5 %copy-start = (f32[256,256]{0,1:T(8,128)S(1)}, f32[256,256]{0,1:T(8,128)}, u32[]{:S(2)}) copy-start(f32[256,256]{0,1:T(8,128)} %all-reduce.6.cloned.1.call-done) | copy-start | bytes 786436
  258.4 189.7 %all-reduce.8.cloned.1.call-start = ((), (), s32[]{:S(2)}) async-start(), calls=%async_computation.5 | async-start | bytes 524288 | tf_op jit(solution)/shard_map/psum | solution.py:14
  388.4 117.8 %all-gather.7.cloned.1.call-start = ((), (), s32[]{:S(2)}) async-start(), calls=%async_computation.6 | async-start | bytes 4456448 | tf_op jit(solution)/shard_map/all_gather | solution.py:73
  448.2 120.8 %copy-start.2 = (f32[256,256]{0,1:T(8,128)S(1)}, f32[256,256]{0,1:T(8,128)}, u32[]{:S(2)}) copy-start(f32[256,256]{0,1:T(8,128)} %all-reduce.8.cloned.1.call-done) | copy-start | bytes 786436
  448.2 189.3 %all-reduce.10.cloned.1.call-start = ((), (), s32[]{:S(2)}) async-start(), calls=%async_computation.7 | async-start | bytes 524288 | tf_op jit(solution)/shard_map/psum | solution.py:14
  577.8 117.9 %all-gather.9.cloned.1.call-start = ((), (), s32[]{:S(2)}) async-start(), calls=%async_computation.8 | async-start | bytes 4456448 | tf_op jit(solution)/shard_map/all_gather | solution.py:73
  637.5 121.2 %copy-start.3 = (f32[256,256]{0,1:T(8,128)S(1)}, f32[256,256]{0,1:T(8,128)}, u32[]{:S(2)}) copy-start(f32[256,256]{0,1:T(8,128)} %all-reduce.10.cloned.1.call-done) | copy-start | bytes 786436
  637.5 190.3 %all-reduce.12.cloned.1.call-start = ((), (), s32[]{:S(2)}) async-start(), calls=%async_computation.9 | async-start | bytes 524288 | tf_op jit(solution)/shard_map/psum | solution.py:14
  768.1 117.9 %all-gather.11.cloned.1.call-start = ((), (), s32[]{:S(2)}) async-start(), calls=%async_computation.10 | async-start | bytes 4456448 | tf_op jit(solution)/shard_map/all_gather | solution.py:73
  827.8 120.6 %copy-start.1 = (f32[256,256]{0,1:T(8,128)S(1)}, f32[256,256]{0,1:T(8,128)}, u32[]{:S(2)}) copy-start(f32[256,256]{0,1:T(8,128)} %all-reduce.12.cloned.1.call-done) | copy-start | bytes 786436
Sparse Core Ops, SparseCore 0:
  109.8 86.6 reduce-scatter.1
  198.8 59.5 all-reduce.5
  260.5 55.9 all-gather.4
  388.5 59.6 all-reduce.7
  450.1 55.9 all-gather.6
  577.9 59.5 all-reduce.9
  639.6 55.9 all-gather.8
  768.3 59.5 all-reduce.11
  830.0 55.9 all-gather.10
where the time goes:
time: 972 us; the launch traced here: 964 us
  waiting for transfers between devices  555 us (57%)
  other arithmetic  228 us (23%)
  local copies, waits for them, and re-layouts  62 us (6%)
  blocking collectives  54.3 us (6%)
  matrix products  42.7 us (4%)
  between operations  20.3 us (2%)
    psum x4, waiting for transfers between devices, spread(): return lax.psum(jnp.where(mine, array, jnp.zeros_like(array)), axis)  239 us
    all_gather x4, waiting for transfers between devices, shards(): full_column = lax.all_gather(column, 'leaf', axis=0, tiled=True)  230 us
    another operation x27, other arithmetic, shards(): factor = jnp.linalg.cholesky(full_column[pivot_start:pivot_start + TILE])  138 us
    reduce_scatter x1, waiting for transfers between devices, shards(): lax.psum_scatter(jnp.einsum('ft,tbc->fbc', picked, column_tiles, precisio...  85.6 us
    another operation x9, other arithmetic, finish_rows(): lax.linalg.triangular_solve(factor, block, left_side=False, lower=True, t...  79.3 us
    all_to_all x1, blocking collectives, shards(): lax.all_to_all(placed, 'panel', split_axis=1, concat_axis=0, tiled=True)  54.3 us
  transfers between devices with their start and end apart: 9, of which 9 were waited for; matrix products, arithmetic and copies ran while one was open for 0% of the time, Pallas kernels for 0%

commit v1 on v0

--- a/solution.py
+++ b/solution.py
@@ -7,6 +7,12 @@
 NF = 4096
 CB = 2048
 STEPS = 4
+
+
+def in_order(blocks, dim):
+    blocks = jnp.moveaxis(blocks, 0, dim)
+    dims = blocks.shape
+    return blocks.reshape(*dims[:dim], dims[dim] * dims[dim + 1], *dims[dim + 2 :])
 
 
 def spread(array, axis, root):
@@ -70,7 +76,19 @@
         pivot_start = pivot_step * TILE
         source = front_block[:, local_start : local_start + TILE]
         column = spread(source, "panel", source_panel)
-        full_column = lax.all_gather(column, "leaf", axis=0, tiled=True)
+        devices = lax.axis_size("leaf")
+        pairs = [(i, (i + 1) % devices) for i in range(devices)]
+        back = [(b, a) for a, b in pairs]
+        lower, upper = ([], [])
+        for hop in range(devices - 1):
+            if hop % 2 == 0:
+                lower.append(lax.ppermute(lower[-1] if lower else column, "leaf", pairs))
+            else:
+                upper.append(lax.ppermute(upper[-1] if upper else column, "leaf", back))
+        blocks = jnp.stack([*lower[::-1], column, *upper])
+        shift = lax.axis_index("leaf") - len(lower)
+        blocks = blocks[(jnp.arange(devices) - shift) % devices]
+        full_column = in_order(blocks, 0)
         factor = jnp.linalg.cholesky(full_column[pivot_start : pivot_start + TILE])
         own_factor = finish_rows(column, global_rows, factor, pivot_start)
         col_factor = finish_rows(

time: 972 us -> 1160 us (1.19)
  starting transfers between devices: 1.13 us -> 164 us
  local copies, waits for them, and re-layouts: 62 us -> 162 us
  waiting for transfers between devices: 555 us -> 482 us
    all_gather x4 -> x0, waiting for transfers between devices: 230 us -> none  [shards(): full_column = lax.all_gather(column, 'leaf', axis=0, tiled=True)]
    ppermute x0 -> x60, waiting for transfers between devices: none -> 175 us  [the longest x32 173 us: shards(): lower.append(lax.ppermute(lower[-1] if lower else column, 'leaf', pairs))]
    ppermute x0 -> x60, starting transfers between devices: none -> 164 us  [the longest x28 158 us: shards(): upper.append(lax.ppermute(upper[-1] if upper else column, 'leaf', back))]
    unnamed x15 -> x78, local copies, waits for them, and re-layouts: 13.4 us -> 57.7 us
    gather x0 -> x8, local copies, waits for them, and re-layouts: none -> 41.5 us  [shards(): blocks = blocks[(jnp.arange(devices) - shift) % devices]]
    psum x4, waiting for transfers between devices: 239 us -> 222 us  [spread(): return lax.psum(jnp.where(mine, array, jnp.zeros_like(array)), axis)]
  transfers between devices with their start and end apart: 9 -> 65, of which waited for: 9 -> 46; matrix products, arithmetic and copies ran while one was open for 0% -> 5% of each run, Pallas kernels for 0% -> 0%
where the time goes in v1:
time: 1160 us; the launch traced here: 1150 us
  waiting for transfers between devices  482 us (42%)
  other arithmetic  228 us (20%)
  starting transfers between devices  164 us (14%)
  local copies, waits for them, and re-layouts  162 us (14%)
  blocking collectives  54.2 us (5%)
  matrix products  43.8 us (4%)
  between operations  20.1 us (2%)
    psum x4, waiting for transfers between devices, spread(): return lax.psum(jnp.where(mine, array, jnp.zeros_like(array)), axis)  222 us
    ppermute x32, waiting for transfers between devices, shards(): lower.append(lax.ppermute(lower[-1] if lower else column, 'leaf', pairs))  173 us
    ppermute x28, starting transfers between devices, shards(): upper.append(lax.ppermute(upper[-1] if upper else column, 'leaf', back))  158 us
    another operation x27, other arithmetic, shards(): factor = jnp.linalg.cholesky(full_column[pivot_start:pivot_start + TILE])  138 us
    reduce_scatter x1, waiting for transfers between devices, shards(): lax.psum_scatter(jnp.einsum('ft,tbc->fbc', picked, column_tiles, precisio...  85.3 us
    another operation x9, other arithmetic, finish_rows(): lax.linalg.triangular_solve(factor, block, left_side=False, lower=True, t...  79.8 us
    unnamed x78, local copies, waits for them, and re-layouts  57.7 us
    all_to_all x1, blocking collectives, shards(): lax.all_to_all(placed, 'panel', split_axis=1, concat_axis=0, tiled=True)  54.2 us
  transfers between devices with their start and end apart: 65, of which 46 were waited for; matrix products, arithmetic and copies ran while one was open for 5% of the time, Pallas kernels for 0%

profile of v1, /device:TPU:0, one launch (start us, length us, event | category | flops | bytes accessed | tf_op | source)
XLA Modules:
  0.0 1154.6 jit_solution(13844293767801567548)
XLA Ops:
  6.5 11.5 fusion.5
  33.1 54.2 %all_to_all.15 = f32[256,8,512]{2,0,1:T(8,128)S(1)} all-to-all(f32[256,8,512]{2,0,1:T(8,128)S(1)} %copy.48), channel_id=1, replica_groups=mesh['leaf'=16,'panel'=8] {'panel'}, dimensions={1} | all-to-all | bytes 8388608 | tf_op jit(solution)/shard_map/all_to_all | solution.py:58
  101.2 8.9 copy.51
  111.4 85.3 %reduce-scatter.2.cloned.1.call-done = f32[256,512]{0,1:T(8,128)} async-done(((f32[4096,512]{0,1:T(8,128)}), f32[256,512]{0,1:T(8,128)}) %reduce-scatter.2.cloned.1.call-update) | async-done | bytes 524304 | tf_op jit(solution)/shard_map/reduce_scatter | solution.py:62
  198.6 60.1 %all-reduce.6.cloned.1.call-done = f32[256,256]{0,1:T(8,128)} async-done(((f32[256,256]{0,1:T(8,128)}), f32[256,256]{0,1:T(8,128)}) %all-reduce.6.cloned.1.call-update) | async-done | bytes 262160 | tf_op jit(solution)/shard_map/psum | solution.py:20
  372.5 11.7 %cholesky.214 = f32[128,128]{1,0:T(8,128)S(1)} custom-call(f32[128,128]{1,0:T(8,128)S(1)} %cholesky.346), custom_call_target="Cholesky" | custom-call | tf_op jit(solution)/shard_map/jit(cholesky)/cholesky | solution.py:92
  384.3 9.8 custom-call.23
  394.6 11.7 %cholesky.231 = f32[128,128]{1,0:T(8,128)S(1)} custom-call(f32[128,128]{1,0:T(8,128)S(1)} %convolution_subtract_fusion.15), custom_call_target="Cholesky" | custom-call | tf_op jit(solution)/shard_map/jit(cholesky)/cholesky | solution.py:92
  412.5 19.8 %custom-call.24 = f32[2,128,128]{1,2,0:T(8,128)S(1)} custom-call(f32[2,128,128]{2,1,0:T(8,128)S(1)} %get-tuple-element.110), custom_call_target="InvertDiagBlocksLowerTriangular" | custom-call | tf_op jit(solution)/shard_map/triangular_solve/custom-call.0 | solution.py:24
  442.1 53.8 %all-reduce.8.cloned.1.call-done = f32[256,256]{0,1:T(8,128)} async-done(((f32[256,256]{0,1:T(8,128)}), f32[256,256]{0,1:T(8,128)}) %all-reduce.8.cloned.1.call-update) | async-done | bytes 262160 | tf_op jit(solution)/shard_map/psum | solution.py:20
  609.0 11.7 %cholesky.248 = f32[128,128]{1,0:T(8,128)S(1)} custom-call(f32[128,128]{1,0:T(8,128)S(1)} %cholesky.349), custom_call_target="Cholesky" | custom-call | tf_op jit(solution)/shard_map/jit(cholesky)/cholesky | solution.py:92
  620.8 9.8 custom-call.26
  631.1 11.7 %cholesky.265 = f32[128,128]{1,0:T(8,128)S(1)} custom-call(f32[128,128]{1,0:T(8,128)S(1)} %convolution_subtract_fusion.14), custom_call_target="Cholesky" | custom-call | tf_op jit(solution)/shard_map/jit(cholesky)/cholesky | solution.py:92
  649.5 20.1 %custom-call.27 = f32[2,128,128]{1,2,0:T(8,128)S(1)} custom-call(f32[2,128,128]{2,1,0:T(8,128)S(1)} %get-tuple-element.112), custom_call_target="InvertDiagBlocksLowerTriangular" | custom-call | tf_op jit(solution)/shard_map/triangular_solve/custom-call.0 | solution.py:24
  678.6 53.8 %all-reduce.10.cloned.1.call-done = f32[256,256]{0,1:T(8,128)} async-done(((f32[256,256]{0,1:T(8,128)}), f32[256,256]{0,1:T(8,128)}) %all-reduce.10.cloned.1.call-update) | async-done | bytes 262160 | tf_op jit(solution)/shard_map/psum | solution.py:20
  845.6 11.7 %cholesky.282 = f32[128,128]{1,0:T(8,128)S(1)} custom-call(f32[128,128]{1,0:T(8,128)S(1)} %cholesky.352), custom_call_target="Cholesky" | custom-call | tf_op jit(solution)/shard_map/jit(cholesky)/cholesky | solution.py:92
  857.3 9.8 custom-call.29
  867.6 11.7 %cholesky.299 = f32[128,128]{1,0:T(8,128)S(1)} custom-call(f32[128,128]{1,0:T(8,128)S(1)} %convolution_subtract_fusion.13), custom_call_target="Cholesky" | custom-call | tf_op jit(solution)/shard_map/jit(cholesky)/cholesky | solution.py:92
  886.0 19.9 %custom-call.30 = f32[2,128,128]{1,2,0:T(8,128)S(1)} custom-call(f32[2,128,128]{2,1,0:T(8,128)S(1)} %get-tuple-element.114), custom_call_target="InvertDiagBlocksLowerTriangular" | custom-call | tf_op jit(solution)/shard_map/triangular_solve/custom-call.0 | solution.py:24
  915.6 53.9 %all-reduce.12.cloned.1.call-done = f32[256,256]{0,1:T(8,128)} async-done(((f32[256,256]{0,1:T(8,128)}), f32[256,256]{0,1:T(8,128)}) %all-reduce.12.cloned.1.call-update) | async-done | bytes 262160 | tf_op jit(solution)/shard_map/psum | solution.py:20
  1078.2 11.7 %cholesky.316 = f32[128,128]{1,0:T(8,128)S(1)} custom-call(f32[128,128]{1,0:T(8,128)S(1)} %cholesky.355), custom_call_target="Cholesky" | custom-call | tf_op jit(solution)/shard_map/jit(cholesky)/cholesky | solution.py:92
  1090.0 9.8 custom-call.32
  1100.2 11.7 %cholesky.333 = f32[128,128]{1,0:T(8,128)S(1)} custom-call(f32[128,128]{1,0:T(8,128)S(1)} %convolution_subtract_fusion.12), custom_call_target="Cholesky" | custom-call | tf_op jit(solution)/shard_map/jit(cholesky)/cholesky | solution.py:92
  1118.6 19.8 %custom-call.33 = f32[2,128,128]{1,2,0:T(8,128)S(1)} custom-call(f32[2,128,128]{2,1,0:T(8,128)S(1)} %get-tuple-element.116), custom_call_target="InvertDiagBlocksLowerTriangular" | custom-call | tf_op jit(solution)/shard_map/triangular_solve/custom-call.0 | solution.py:24
  (396 shorter events, 556.1 us)
Async XLA Ops:
  6.5 190.1 %reduce-scatter.2.cloned.1.call-start = ((), (), s32[]{:S(2)}) async-start(), calls=%async_computation.2 | async-start | bytes 8912896 | tf_op jit(solution)/shard_map/reduce_scatter | solution.py:62
  110.2 148.5 %all-reduce.6.cloned.1.call-start = ((), (), s32[]{:S(2)}) async-start(), calls=%async_computation.3 | async-start | bytes 524288 | tf_op jit(solution)/shard_map/psum | solution.py:20
  198.5 297.4 %all-reduce.8.cloned.1.call-start = ((), (), s32[]{:S(2)}) async-start(), calls=%async_computation.4 | async-start | bytes 524288 | tf_op jit(solution)/shard_map/psum | solution.py:20
  298.6 11.8 %collective-permute-start.4 = (f32[256,256]{0,1:T(8,128)S(1)}, f32[256,256]{0,1:T(8,128)S(1)}, u32[]{:S(2)}, u32[]{:S(2)}) collective-permute-start(f32[256,256]{0,1:T(8,128)S(1)} %collective-permute-done.3), channel_id=1, source_target_pairs={{0,8},{8,16},{16,24},{24,32},{32,40},{40,48},{48,56},{56,64},{64,7... | collective-permute-start | bytes 786440 | tf_op jit(solution)/shard_map/ppermute | solution.py:85
  298.7 12.0 %collective-permute-start.11 = (f32[256,256]{0,1:T(8,128)S(1)}, f32[256,256]{0,1:T(8,128)S(1)}, u32[]{:S(2)}, u32[]{:S(2)}) collective-permute-start(f32[256,256]{0,1:T(8,128)S(1)} %collective-permute-done.10), channel_id=1, source_target_pairs={{8,0},{16,8},{24,16},{32,24},{40,32},{48,40},{56,48},{64,56},{72,6... | collective-permute-start | bytes 786440 | tf_op jit(solution)/shard_map/ppermute | solution.py:87
  310.4 12.5 %collective-permute-start.5 = (f32[256,256]{0,1:T(8,128)S(1)}, f32[256,256]{0,1:T(8,128)}, u32[]{:S(2)}, u32[]{:S(2)}) collective-permute-start(f32[256,256]{0,1:T(8,128)S(1)} %collective-permute-done.4), channel_id=1, source_target_pairs={{0,8},{8,16},{16,24},{24,32},{32,40},{40,48},{48,56},{56,64},{64,7... | collective-permute-start | bytes 786440 | tf_op jit(solution)/shard_map/ppermute | solution.py:85
  310.7 12.2 %collective-permute-start.12 = (f32[256,256]{0,1:T(8,128)S(1)}, f32[256,256]{0,1:T(8,128)S(1)}, u32[]{:S(2)}, u32[]{:S(2)}) collective-permute-start(f32[256,256]{0,1:T(8,128)S(1)} %collective-permute-done.11), channel_id=1, source_target_pairs={{8,0},{16,8},{24,16},{32,24},{40,32},{48,40},{56,48},{64,56},{72,6... | collective-permute-start | bytes 786440 | tf_op jit(solution)/shard_map/ppermute | solution.py:87
  322.9 11.9 %collective-permute-start.6 = (f32[256,256]{0,1:T(8,128)}, f32[256,256]{0,1:T(8,128)}, u32[]{:S(2)}, u32[]{:S(2)}) collective-permute-start(f32[256,256]{0,1:T(8,128)} %collective-permute-done.5), channel_id=1, source_target_pairs={{0,8},{8,16},{16,24},{24,32},{32,40},{40,48},{48,56},{56,64},{64,7... | collective-permute-start | bytes 786440 | tf_op jit(solution)/shard_map/ppermute | solution.py:85
  322.9 12.6 %collective-permute-start.13 = (f32[256,256]{0,1:T(8,128)S(1)}, f32[256,256]{0,1:T(8,128)}, u32[]{:S(2)}, u32[]{:S(2)}) collective-permute-start(f32[256,256]{0,1:T(8,128)S(1)} %collective-permute-done.12), channel_id=1, source_target_pairs={{8,0},{16,8},{24,16},{32,24},{40,32},{48,40},{56,48},{64,56},{72,6... | collective-permute-start | bytes 786440 | tf_op jit(solution)/shard_map/ppermute | solution.py:87
  335.5 23.8 %collective-permute-start.14 = (f32[256,256]{0,1:T(8,128)}, f32[256,256]{0,1:T(8,128)S(1)}, u32[]{:S(2)}, u32[]{:S(2)}) collective-permute-start(f32[256,256]{0,1:T(8,128)} %collective-permute-done.13), channel_id=1, source_target_pairs={{8,0},{16,8},{24,16},{32,24},{40,32},{48,40},{56,48},{64,56},{72,6... | collective-permute-start | bytes 786440 | tf_op jit(solution)/shard_map/ppermute | solution.py:87
  442.0 290.4 %all-reduce.10.cloned.1.call-start = ((), (), s32[]{:S(2)}) async-start(), calls=%async_computation.5 | async-start | bytes 524288 | tf_op jit(solution)/shard_map/psum | solution.py:20
  535.9 12.0 %collective-permute-start.26 = (f32[256,256]{0,1:T(8,128)S(1)}, f32[256,256]{0,1:T(8,128)S(1)}, u32[]{:S(2)}, u32[]{:S(2)}) collective-permute-start(f32[256,256]{0,1:T(8,128)S(1)} %collective-permute-done.25), channel_id=1, source_target_pairs={{8,0},{16,8},{24,16},{32,24},{40,32},{48,40},{56,48},{64,56},{72,6... | collective-permute-start | bytes 786440 | tf_op jit(solution)/shard_map/ppermute | solution.py:87
  547.6 12.1 %collective-permute-start.20 = (f32[256,256]{0,1:T(8,128)S(1)}, f32[256,256]{0,1:T(8,128)S(1)}, u32[]{:S(2)}, u32[]{:S(2)}) collective-permute-start(f32[256,256]{0,1:T(8,128)S(1)} %collective-permute-done.19), channel_id=1, source_target_pairs={{0,8},{8,16},{16,24},{24,32},{32,40},{40,48},{48,56},{56,64},{64,7... | collective-permute-start | bytes 786440 | tf_op jit(solution)/shard_map/ppermute | solution.py:85
  547.9 11.8 %collective-permute-start.27 = (f32[256,256]{0,1:T(8,128)S(1)}, f32[256,256]{0,1:T(8,128)S(1)}, u32[]{:S(2)}, u32[]{:S(2)}) collective-permute-start(f32[256,256]{0,1:T(8,128)S(1)} %collective-permute-done.26), channel_id=1, source_target_pairs={{8,0},{16,8},{24,16},{32,24},{40,32},{48,40},{56,48},{64,56},{72,6... | collective-permute-start | bytes 786440 | tf_op jit(solution)/shard_map/ppermute | solution.py:87
  571.3 24.5 %collective-permute-start.29 = (f32[256,256]{0,1:T(8,128)}, f32[256,256]{0,1:T(8,128)S(1)}, u32[]{:S(2)}, u32[]{:S(2)}) collective-permute-start(f32[256,256]{0,1:T(8,128)} %collective-permute-done.28), channel_id=1, source_target_pairs={{8,0},{16,8},{24,16},{32,24},{40,32},{48,40},{56,48},{64,56},{72,6... | collective-permute-start | bytes 786440 | tf_op jit(solution)/shard_map/ppermute | solution.py:87
  678.6 290.9 %all-reduce.12.cloned.1.call-start = ((), (), s32[]{:S(2)}) async-start(), calls=%async_computation.6 | async-start | bytes 524288 | tf_op jit(solution)/shard_map/psum | solution.py:20
  772.5 12.0 %collective-permute-start.41 = (f32[256,256]{0,1:T(8,128)S(1)}, f32[256,256]{0,1:T(8,128)S(1)}, u32[]{:S(2)}, u32[]{:S(2)}) collective-permute-start(f32[256,256]{0,1:T(8,128)S(1)} %collective-permute-done.40), channel_id=1, source_target_pairs={{8,0},{16,8},{24,16},{32,24},{40,32},{48,40},{56,48},{64,56},{72,6... | collective-permute-start | bytes 786440 | tf_op jit(solution)/shard_map/ppermute | solution.py:87
  784.1 12.1 %collective-permute-start.35 = (f32[256,256]{0,1:T(8,128)S(1)}, f32[256,256]{0,1:T(8,128)S(1)}, u32[]{:S(2)}, u32[]{:S(2)}) collective-permute-start(f32[256,256]{0,1:T(8,128)S(1)} %collective-permute-done.34), channel_id=1, source_target_pairs={{0,8},{8,16},{16,24},{24,32},{32,40},{40,48},{48,56},{56,64},{64,7... | collective-permute-start | bytes 786440 | tf_op jit(solution)/shard_map/ppermute | solution.py:85
  784.5 11.8 %collective-permute-start.42 = (f32[256,256]{0,1:T(8,128)S(1)}, f32[256,256]{0,1:T(8,128)S(1)}, u32[]{:S(2)}, u32[]{:S(2)}) collective-permute-start(f32[256,256]{0,1:T(8,128)S(1)} %collective-permute-done.41), channel_id=1, source_target_pairs={{8,0},{16,8},{24,16},{32,24},{40,32},{48,40},{56,48},{64,56},{72,6... | collective-permute-start | bytes 786440 | tf_op jit(solution)/shard_map/ppermute | solution.py:87
  807.8 24.5 %collective-permute-start.44 = (f32[256,256]{0,1:T(8,128)}, f32[256,256]{0,1:T(8,128)S(1)}, u32[]{:S(2)}, u32[]{:S(2)}) collective-permute-start(f32[256,256]{0,1:T(8,128)} %collective-permute-done.43), channel_id=1, source_target_pairs={{8,0},{16,8},{24,16},{32,24},{40,32},{48,40},{56,48},{64,56},{72,6... | collective-permute-start | bytes 786440 | tf_op jit(solution)/shard_map/ppermute | solution.py:87
  1009.5 12.0 %collective-permute-start.56 = (f32[256,256]{0,1:T(8,128)S(1)}, f32[256,256]{0,1:T(8,128)S(1)}, u32[]{:S(2)}, u32[]{:S(2)}) collective-permute-start(f32[256,256]{0,1:T(8,128)S(1)} %collective-permute-done.55), channel_id=1, source_target_pairs={{8,0},{16,8},{24,16},{32,24},{40,32},{48,40},{56,48},{64,56},{72,6... | collective-permute-start | bytes 786440 | tf_op jit(solution)/shard_map/ppermute | solution.py:87
  1021.2 12.1 %collective-permute-start.50 = (f32[256,256]{0,1:T(8,128)S(1)}, f32[256,256]{0,1:T(8,128)S(1)}, u32[]{:S(2)}, u32[]{:S(2)}) collective-permute-start(f32[256,256]{0,1:T(8,128)S(1)} %collective-permute-done.49), channel_id=1, source_target_pairs={{0,8},{8,16},{16,24},{24,32},{32,40},{40,48},{48,56},{56,64},{64,7... | collective-permute-start | bytes 786440 | tf_op jit(solution)/shard_map/ppermute | solution.py:85
  1021.5 11.8 %collective-permute-start.57 = (f32[256,256]{0,1:T(8,128)S(1)}, f32[256,256]{0,1:T(8,128)S(1)}, u32[]{:S(2)}, u32[]{:S(2)}) collective-permute-start(f32[256,256]{0,1:T(8,128)S(1)} %collective-permute-done.56), channel_id=1, source_target_pairs={{8,0},{16,8},{24,16},{32,24},{40,32},{48,40},{56,48},{64,56},{72,6... | collective-permute-start | bytes 786440 | tf_op jit(solution)/shard_map/ppermute | solution.py:87
  1044.7 20.2 %collective-permute-start.59 = (f32[256,256]{0,1:T(8,128)S(1)}, f32[256,256]{0,1:T(8,128)S(1)}, u32[]{:S(2)}, u32[]{:S(2)}) collective-permute-start(f32[256,256]{0,1:T(8,128)S(1)} %collective-permute-done.58), channel_id=1, source_target_pairs={{8,0},{16,8},{24,16},{32,24},{40,32},{48,40},{56,48},{64,56},{72,6... | collective-permute-start | bytes 786440 | tf_op jit(solution)/shard_map/ppermute | solution.py:87
  (49 other events, 799.3 us)
Sparse Core Ops, SparseCore 0:
  110.3 86.3 reduce-scatter.1
  199.0 59.6 all-reduce.5
  442.2 53.7 all-reduce.7
  678.7 53.7 all-reduce.9
  915.7 53.7 all-reduce.11
